TPU v7x, 256 devices: a whole 4x4x8 slice. The times are simulated.
256 devices in a mesh: row: 64 (over x, z_hi, y), col: 4 (over z_lo, core).
Axes of the slice: x: 4, y: 4, z: 8 (z_hi: 4, z_lo: 2; z = z_hi * 2 + z_lo), core: 2. Of those that a mesh axis runs over, the one named last changes fastest.
Arguments:
- img_hidden: bfloat16 [8, 1536, 2432], P(None, 'row', 'col'), may hold values from -6 to 6
- txt_hidden: bfloat16 [8, 128, 2432], P(None, 'row', 'col'), may hold values from -6 to 6
- latent: float32 [8, 1536, 64], P(None, 'row'), may hold values from -6 to 6
- img_mod: float32 [8, 5, 2432], replicated, may hold values from -4 to 4
- txt_mod: float32 [8, 2, 2432], replicated, may hold values from -4 to 4
- qkv_weight: bfloat16 [3, 2432, 2048], P(None, None, 'col'), may hold values from -0.125 to 0.125
- txt_kv_weight: bfloat16 [2, 2432, 2048], P(None, None, 'col'), may hold values from -0.125 to 0.125
- out_weight: bfloat16 [2048, 2432], P('col', 'row'), may hold values from -0.125 to 0.125
- final_weight: bfloat16 [2432, 64], P('col'), may hold values from -0.125 to 0.125
- qk_gains: float32 [3, 64], replicated, may hold values from 1.5 to 9
- txt_len: int32 [8], replicated, may hold values from 1 to 128, as said below
- step_idx: int32 [8], replicated, may hold values from 1 to 28
Outputs:
- advanced: float32 [8, 1536, 64], P(None, 'row')
- denoised: float32 [8, 1536, 64], P(None, 'row')
Inputs may be any that keep to these rules, and one draw needn't show every extreme that they name: `txt_len`: some request has all 128 text tokens live.
All inputs are finite; a program needn't handle non-finite values.
Results may differ from a plain program's by a relative error of at most 0.0044.
The roundings to bfloat16 on the way count: a program that leaves them out, or rounds other values in their place, can miss the bound.
Values may be sent and summed in bfloat16 or wider, within the bound.
No kernel may reach another device: no remote copies, remote signals or barrier semaphores. Data moves between devices by JAX's collectives and lax.ppermute only.
A program may use at most 128 MiB of HBM per device.

v0:
```python
import jax
import jax.numpy as jnp
from jax import lax
from jax.sharding import PartitionSpec as P

D = 2432
HD = 64
STEPS = 28
eps_norm = 1e-06
neg_fill = -1e30


def layer_norm(values):
    average = jnp.mean(values, -1, keepdims=True)
    centred = values - average
    variance = jnp.mean(centred * centred, -1, keepdims=True)
    return centred * lax.rsqrt(variance + eps_norm)


def rms_heads(values, scaling):
    reshaped = values.reshape(values.shape[:-1] + (values.shape[-1] // HD, HD))
    inverse = lax.rsqrt(jnp.mean(reshaped * reshaped, -1, keepdims=True) + eps_norm)
    return (reshaped * inverse * scaling).astype(jnp.bfloat16)


def sigma_at(indices):
    fraction = indices.astype(jnp.float32) / STEPS
    return 3.0 * fraction / (1.0 + 2.0 * fraction)


def attend_all(queries, key_rows, value_rows, allowed):
    scores = jnp.einsum(
        "rqhd,rkhd->rqhk", queries, key_rows, preferred_element_type=jnp.float32
    ) * HD ** (-0.5)
    scores = jnp.where(allowed[:, None, None, :], scores, neg_fill)
    top_score = jnp.max(scores, -1, keepdims=True)
    exp_scores = jnp.where(allowed[:, None, None, :], jnp.exp(scores - top_score), 0.0)
    row_total = jnp.sum(exp_scores, -1)
    weighted = jnp.einsum(
        "rqhk,rkhd->rqhd",
        exp_scores.astype(jnp.bfloat16),
        value_rows,
        preferred_element_type=jnp.float32,
    )
    return (weighted / row_total[..., None]).astype(jnp.bfloat16)


def per_device(
    img_hidden,
    txt_hidden,
    latent,
    img_mod,
    txt_mod,
    qkv_weight,
    txt_kv_weight,
    out_weight,
    final_weight,
    qk_gains,
    txt_len,
    step_idx,
):
    requests = img_hidden.shape[0]
    patches = img_hidden.shape[1]
    text_rows = txt_hidden.shape[1]
    cols_local = qkv_weight.shape[2]
    heads_local = cols_local // HD
    block_len = patches + text_rows
    img_full, txt_full = (
        lax.all_gather(img_hidden, "col", axis=2, tiled=True),
        lax.all_gather(txt_hidden, "col", axis=2, tiled=True),
    )
    img_wide = img_full.astype(jnp.float32)
    normed = (layer_norm(img_wide) * (1.0 + img_mod[:, 1:2, :]) + img_mod[:, 0:1, :]).astype(
        jnp.bfloat16
    )
    flat_rows = normed.reshape(requests * patches, D)
    projected = jnp.einsum("td,cde->cte", flat_rows, qkv_weight, preferred_element_type=jnp.float32)
    queries = rms_heads(projected[0], qk_gains[0]).reshape(requests, patches, heads_local, HD)
    img_keys = rms_heads(projected[1], qk_gains[1]).reshape(requests, patches, heads_local, HD)
    img_values = projected[2].astype(jnp.bfloat16).reshape(requests, patches, heads_local, HD)
    text_normed = (
        layer_norm(txt_full.astype(jnp.float32)) * (1.0 + txt_mod[:, 1:2, :]) + txt_mod[:, 0:1, :]
    ).astype(jnp.bfloat16)
    text_proj = jnp.einsum(
        "rtd,cde->crte", text_normed, txt_kv_weight, preferred_element_type=jnp.float32
    )
    text_keys = rms_heads(text_proj[0], qk_gains[2])
    text_values = text_proj[1].astype(jnp.bfloat16).reshape(requests, text_rows, heads_local, HD)
    key_rows = jnp.concatenate([img_keys, text_keys], 1)
    value_rows = jnp.concatenate([img_values, text_values], 1)
    key_flat = key_rows.reshape(requests, block_len, cols_local)
    value_flat = value_rows.reshape(requests, block_len, cols_local)
    all_keys, all_values = (
        lax.all_gather(key_flat, "row", axis=1, tiled=True),
        lax.all_gather(value_flat, "row", axis=1, tiled=True),
    )
    key_count = all_keys.shape[1]
    positions = jnp.arange(key_count, dtype=jnp.int32)
    gathered_keys = all_keys.reshape(requests, key_count, heads_local, HD)
    gathered_values = all_values.reshape(requests, key_count, heads_local, HD)
    within = positions % block_len
    source = positions // block_len
    text_pos = source * text_rows + within - patches
    attended = attend_all(
        queries,
        gathered_keys,
        gathered_values,
        (within[None, :] < patches) | (text_pos[None, :] < txt_len[:, None]),
    ).reshape(requests * patches, cols_local)
    partial_value = jnp.dot(
        attended,
        lax.all_gather(out_weight, "row", axis=1, tiled=True),
        preferred_element_type=jnp.float32,
    )
    slab_width = img_hidden.shape[2]
    col_index = lax.axis_index("col")
    shared_sum = lax.psum_scatter(partial_value, "col", scatter_dimension=1, tiled=True)
    col_mods = lax.dynamic_slice_in_dim(img_mod, col_index * slab_width, slab_width, 2)
    mixed = img_hidden.astype(jnp.float32) + col_mods[:, 2:3, :] * shared_sum.reshape(
        requests, patches, slab_width
    )
    row_sums, squares = lax.psum((jnp.sum(mixed, -1), jnp.sum(mixed * mixed, -1)), "col")
    row_mean = row_sums / D
    spread = squares / D - row_mean * row_mean
    scaled = (mixed - row_mean[..., None]) * lax.rsqrt(spread[..., None] + eps_norm)
    modulated = (scaled * (1.0 + col_mods[:, 4:5, :]) + col_mods[:, 3:4, :]).astype(jnp.bfloat16)
    velocity = lax.psum(
        jnp.dot(
            modulated.reshape(requests * patches, slab_width),
            final_weight,
            preferred_element_type=jnp.float32,
        ),
        "col",
    )
    velocity = velocity.reshape(requests, patches, latent.shape[2])
    sigma_now = sigma_at(step_idx)[:, None, None]
    sigma_next = sigma_at(step_idx - 1)[:, None, None]
    advanced = latent + (sigma_next - sigma_now) * velocity
    denoised = latent - sigma_now * velocity
    return (advanced, denoised)


def solution(mesh):
    in_specs = (
        P(None, "row", "col"),
        P(None, "row", "col"),
        P(None, "row", None),
        P(),
        P(),
        P(None, None, "col"),
        P(None, None, "col"),
        P("col", "row"),
        P("col", None),
        P(),
        P(),
        P(),
    )
    out_specs = (P(None, "row", None), P(None, "row", None))
    return jax.shard_map(
        per_device, mesh=mesh, in_specs=in_specs, out_specs=out_specs, check_vma=False
    )
```

profile of v0, /device:TPU:1, one launch (start us, length us, event | category | flops | bytes accessed | tf_op | source)
XLA Modules:
  0.0 487.1 jit_solution(12438980188880885017)
XLA Ops:
  7.2 0.7 all-gather.9.cloned.1.call-update
  8.0 1.0 copy.78
  9.0 12.9 %all_gather.16 = bf16[8,2,2432]{0,1,2:T(2,128)(2,1)S(1)} all-gather(bf16[8,2,608]{0,1,2:T(2,128)(2,1)S(1)} %copy.78), channel_id=1, replica_groups=mesh['row'=64,'col'=4] {'col'}, dimensions={2}, use_global_device_ids=true | all-gather | bytes 97280 | tf_op jit(solution)/shard_map/all_gather | solution.py:70
  21.9 1.1 copy.79
  23.0 0.1 convert_reduce_fusion.1
  23.1 0.2 fusion.39
  23.3 1.1 fusion.73
  24.4 3.2 fusion.24
  28.1 0.8 copy.76
  28.9 35.2 %all_gather.15 = bf16[8,24,2432]{1,0,2:T(8,128)(2,1)} all-gather(bf16[8,24,608]{1,0,2:T(8,128)(2,1)S(1)} %copy.76), channel_id=1, replica_groups=mesh['row'=64,'col'=4] {'col'}, dimensions={2}, use_global_device_ids=true | all-gather | bytes 1167360 | tf_op jit(solution)/shard_map/all_gather | solution.py:69
  64.1 4.8 copy.77
  69.0 0.2 convert_reduce_fusion
  69.2 0.4 fusion.17
  69.6 0.9 add_bitcast_fusion
  70.5 0.6 fusion.20
  71.1 4.8 convolution_bitcast_fusion.1
  76.0 0.2 slice_multiply_fusion.1
  76.2 0.8 copy-done.2
  77.0 0.2 copy.84
  77.3 0.1 copy.85
  77.4 0.3 mul.258
  77.7 0.2 mul.259
  78.0 0.3 fusion.36
  78.3 0.7 pad_maximum_fusion.1
  79.1 1.0 slice.80
  80.2 0.7 pad_maximum_fusion
  80.9 0.2 reduce-scatter.4.cloned.1.call-start
  81.2 1.1 reshape_squeeze.11
  82.2 0.2 copy.88
  82.7 13.0 %all-gather.9.cloned.1.call-done = bf16[64,38,512]{2,1,0:T(8,128)(2,1)} async-done(((bf16[1,38,512]{2,1,0:T(8,128)(2,1)}), bf16[64,38,512]{2,1,0:T(8,128)(2,1)}) %all-gather.9.cloned.1.call-update) | async-done | bytes 2490384 | tf_op jit(solution)/shard_map/all_gather | solution.py:112
  95.8 2.8 reshape.196
  98.5 137.7 %all-gather.7.cloned.1.call-done = bf16[8,1664,512]{2,0,1:T(8,128)(2,1)} async-done(((bf16[8,26,512]{2,0,1:T(8,128)(2,1)}), bf16[8,1664,512]{2,0,1:T(8,128)(2,1)}) %all-gather.7.cloned.1.call-update) | async-done | bytes 13631504 | tf_op jit(solution)/shard_map/all_gather | solution.py:94
  236.3 19.4 %copy.87 = bf16[8,1664,512]{1,2,0:T(8,128)(2,1)} copy(bf16[8,1664,512]{2,0,1:T(8,128)(2,1)} %all-gather.7.cloned.1.call-done) | data formatting | bytes 27262976 | tf_op jit(solution)/shard_map/all_gather | solution.py:94
  255.7 8.9 %fusion.74 = (f32[8,24,8]{1,2,0:T(8,128)S(1)}, bf16[8,24,8,1664]{3,1,2,0:T(8,128)(2,1)}) fusion(pred[8,1664]{1,0:T(8,128)(4,1)S(1)} %compare_or_fusion, bf16[8,1664,8,64]{1,3,2,0:T(8,128)(2,1)} %bitcast.107, f32[8,24,8,64]{3,2,1,0:T(8,128)} %reshape_squeeze.11, f32[64]{0:T(128)S(1)} %get-tuple-element.23, f32[8,24,8]{1,2,0:T(8,128)S(1)} %copy.89), kind=kOutput, calls=%fused_computation.107 | convolution fusion | flops 342787712 | bytes 19162368 | tf_op jit(solution)/shard_map/sub | solution.py:37
  264.6 122.3 %all-gather.5.cloned.1.call-done = bf16[8,1664,512]{2,0,1:T(8,128)(2,1)} async-done(((bf16[8,26,512]{2,0,1:T(8,128)(2,1)}), bf16[8,1664,512]{2,0,1:T(8,128)(2,1)}) %all-gather.5.cloned.1.call-update) | async-done | bytes 13631504 | tf_op jit(solution)/shard_map/all_gather | solution.py:95
  386.9 19.4 %copy.83 = bf16[8,1664,512]{1,2,0:T(8,128)(2,1)} copy(bf16[8,1664,512]{2,0,1:T(8,128)(2,1)} %all-gather.5.cloned.1.call-done) | data formatting | bytes 27262976 | tf_op jit(solution)/shard_map/all_gather | solution.py:95
  406.3 8.4 %fusion.30 = bf16[8,24,8,64]{3,1,2,0:T(8,128)(2,1)S(1)} fusion(bf16[8,1664,8,64]{1,3,2,0:T(8,128)(2,1)} %bitcast.108, bf16[8,24,8,1664]{3,1,2,0:T(8,128)(2,1)} %get-tuple-element.27, f32[8,24,8]{1,2,0:T(8,128)S(1)} %get-tuple-element.26), kind=kOutput, calls=%fused_computation.28 | convolution fusion | flops 327352320 | bytes 18946048 | tf_op jit(solution)/shard_map/rqhk,rkhd->rqhd/dot_general | solution.py:39
  414.8 0.3 reshape.191
  415.1 2.3 convolution_bitcast_fusion
  417.4 0.9 dynamic-slice_bitcast_fusion.1
  418.2 42.7 %reduce-scatter.4.cloned.1.call-done = f32[608,192]{1,0:T(8,128)} async-done(((f32[2432,192]{1,0:T(8,128)}), f32[608,192]{1,0:T(8,128)}) %reduce-scatter.4.cloned.1.call-update) | async-done | bytes 466960
  461.0 1.3 copy.96
  462.3 0.2 fusion.43
  462.4 5.5 %all-reduce = (f32[8,24]{1,0:T(8,128)S(1)}, f32[8,24]{1,0:T(8,128)S(1)}) all-reduce(f32[8,24]{1,0:T(8,128)S(1)} %get-tuple-element.3, f32[8,24]{1,0:T(8,128)S(1)} %get-tuple-element.2), channel_id=1, replica_groups=mesh['row'=64,'col'=4] {'col'}, use_global_device_ids=true, to_apply=%region_13.14 | all-reduce | flops 384 | bytes 3072 | tf_op jit(solution)/shard_map/psum | solution.py:122
  467.9 0.2 add_convert_fusion
  468.2 0.2 fusion.79
  468.4 11.5 %psum.23 = f32[8,24,64]{2,1,0:T(8,128)S(1)} all-reduce(f32[8,24,64]{2,1,0:T(8,128)S(1)} %bitcast.118), channel_id=1, replica_groups=mesh['row'=64,'col'=4] {'col'}, use_global_device_ids=true, to_apply=%region_14.15 | all-reduce | flops 12288 | bytes 98304 | tf_op jit(solution)/shard_map/psum | solution.py:127
  479.9 0.8 multiply_subtract_fusion
  (51 shorter events, 1.3 us)
Async XLA Ops:
  7.2 461.0 %copy-start = (bf16[608,64]{0,1:T(8,128)(2,1)S(1)}, bf16[608,64]{0,1:T(8,128)(2,1)}, u32[]{:S(2)}) copy-start(bf16[608,64]{0,1:T(8,128)(2,1)} %param.20) | copy-start | bytes 233476
  7.2 20.8 %copy-start.4 = (f32[3,64]{1,0:T(4,128)S(1)}, f32[3,64]{1,0:T(4,128)}, u32[]{:S(2)}) copy-start(f32[3,64]{1,0:T(4,128)} %param.21) | copy-start | bytes 2308
  7.2 20.9 %copy-start.1 = (bf16[8,24,608]{2,1,0:T(8,128)(2,1)S(1)}, bf16[8,24,608]{2,1,0:T(8,128)(2,1)}, u32[]{:S(2)}) copy-start(bf16[8,24,608]{2,1,0:T(8,128)(2,1)} %param.12) | copy-start | bytes 700420
  7.2 88.6 %all-gather.9.cloned.1.call-start = ((), (), s32[]{:S(2)}) async-start(), calls=%async_computation.3 | async-start | bytes 2662400 | tf_op jit(solution)/shard_map/all_gather | solution.py:112
  7.9 228.3 %all-gather.7.cloned.1.call-start = ((), (), s32[]{:S(2)}) async-start(), calls=%async_computation.2 | async-start | bytes 13844480 | tf_op jit(solution)/shard_map/all_gather | solution.py:94
  76.0 1.0 copy-start.2
  77.0 5.7 %copy-start.5 = (s32[8]{0:T(128)S(1)}, s32[8]{0:T(128)}, u32[]{:S(2)}) copy-start(s32[8]{0:T(128)} %param.22) | copy-start | bytes 100
  79.0 307.9 %all-gather.5.cloned.1.call-start = ((), (), s32[]{:S(2)}) async-start(), calls=%async_computation.1 | async-start | bytes 13844480 | tf_op jit(solution)/shard_map/all_gather | solution.py:95
  80.9 380.0 %reduce-scatter.4.cloned.1.call-start = ((), (), s32[]{:S(2)}) async-start(), calls=%async_computation.4 | async-start | bytes 3112960
  414.8 3.5 copy-start.6
  415.0 64.8 %copy-start.3 = (f32[8,24,64]{2,1,0:T(8,128)S(1)}, f32[8,24,64]{2,1,0:T(8,128)}, u32[]{:S(2)}) copy-start(f32[8,24,64]{2,1,0:T(8,128)} %param.14) | copy-start | bytes 147460
Sparse Core Ops, SparseCore 0:
  11.3 84.3 all-gather.8
  99.0 137.1 all-gather.6
  239.6 147.2 all-gather.4
  417.5 43.4 reduce-scatter.3
where the time goes:
time: 489 us; the launch traced here: 487 us
  waiting for transfers between devices  317 us (65%)
  blocking collectives  65 us (13%)
  local copies, waits for them, and re-layouts  56.6 us (12%)
  matrix products  27.8 us (6%)
  between operations  14.2 us (3%)
  other arithmetic  6.71 us (1%)
    all_gather x1, waiting for transfers between devices, per_device(): lax.all_gather(key_flat, 'row', axis=1, tiled=True)  138 us
    all_gather x1, waiting for transfers between devices, per_device(): lax.all_gather(value_flat, 'row', axis=1, tiled=True)  122 us
    unnamed x5, waiting for transfers between devices  43.4 us
    all_gather x1, blocking collectives, per_device(): lax.all_gather(img_hidden, 'col', axis=2, tiled=True)  35.2 us
    all_gather x1, local copies, waits for them, and re-layouts, per_device(): lax.all_gather(key_flat, 'row', axis=1, tiled=True)  19.4 us
    all_gather x1, local copies, waits for them, and re-layouts, per_device(): lax.all_gather(value_flat, 'row', axis=1, tiled=True)  19.4 us
    all_gather x1, waiting for transfers between devices, per_device(): lax.all_gather(out_weight, 'row', axis=1, tiled=True)  13 us
    all_gather x1, blocking collectives, per_device(): lax.all_gather(txt_hidden, 'col', axis=2, tiled=True)  12.9 us
  transfers between devices with their start and end apart: 4, of which 4 were waited for; matrix products, arithmetic and copies ran while one was open for 12% of the time, Pallas kernels for 0%

commit v1 on v0

--- a/solution.py
+++ b/solution.py
@@ -8,6 +8,13 @@
 STEPS = 28
 eps_norm = 1e-06
 neg_fill = -1e30
+
+
+def all_by_exchange(array, axis, dim):
+    count = lax.axis_size(axis)
+    blocks = jnp.stack([array for _ in range(count)])
+    blocks = lax.all_to_all(blocks, axis, split_axis=0, concat_axis=0)
+    return jnp.concatenate(blocks, axis=dim)
 
 
 def layer_norm(values):
@@ -66,7 +73,7 @@
     heads_local = cols_local // HD
     block_len = patches + text_rows
     img_full, txt_full = (
-        lax.all_gather(img_hidden, "col", axis=2, tiled=True),
+        all_by_exchange(img_hidden, "col", 2),
         lax.all_gather(txt_hidden, "col", axis=2, tiled=True),
     )
     img_wide = img_full.astype(jnp.float32)

time: 489 us -> 494 us (1.010)
  blocking collectives: 65 us -> 36.4 us
  waiting for transfers between devices: 317 us -> 344 us
  starting transfers between devices: 0.34 us -> 7.02 us
    all_gather x1 -> x0, blocking collectives: 35.2 us -> none  [per_device(): lax.all_gather(img_hidden, 'col', axis=2, tiled=True)]
    all_gather x1, waiting for transfers between devices: 13 us -> 40.6 us  [per_device(): lax.all_gather(out_weight, 'row', axis=1, tiled=True)]
    all_to_all x0 -> x1, starting transfers between devices: none -> 6.72 us  [all_by_exchange(): blocks = lax.all_to_all(blocks, axis, split_axis=0, concat_axis=0)]
    all_gather x1, blocking collectives: 12.9 us -> 19.4 us  [per_device(): lax.all_gather(txt_hidden, 'col', axis=2, tiled=True)]
  transfers between devices with their start and end apart: 4 -> 5, of which waited for: 4 -> 4; matrix products, arithmetic and copies ran while one was open for 12% -> 11% of each run, Pallas kernels for 0% -> 0%
where the time goes in v1:
time: 494 us; the launch traced here: 493 us
  waiting for transfers between devices  344 us (70%)
  local copies, waits for them, and re-layouts  54.8 us (11%)
  blocking collectives  36.4 us (7%)
  matrix products  27.7 us (6%)
  between operations  14.2 us (3%)
  other arithmetic  8.26 us (2%)
  starting transfers between devices  7.02 us (1%)
    all_gather x1, waiting for transfers between devices, per_device(): lax.all_gather(key_flat, 'row', axis=1, tiled=True)  138 us
    all_gather x1, waiting for transfers between devices, per_device(): lax.all_gather(value_flat, 'row', axis=1, tiled=True)  122 us
    unnamed x5, waiting for transfers between devices  43.5 us
    all_gather x1, waiting for transfers between devices, per_device(): lax.all_gather(out_weight, 'row', axis=1, tiled=True)  40.6 us
    all_gather x1, blocking collectives, per_device(): lax.all_gather(txt_hidden, 'col', axis=2, tiled=True)  19.4 us
    all_gather x1, local copies, waits for them, and re-layouts, per_device(): lax.all_gather(value_flat, 'row', axis=1, tiled=True)  19.4 us
    all_gather x1, local copies, waits for them, and re-layouts, per_device(): lax.all_gather(key_flat, 'row', axis=1, tiled=True)  19.4 us
    psum x1, blocking collectives, per_device(): lax.psum(jnp.dot(modulated.reshape(requests * patches, slab_width), final...  11.5 us
  transfers between devices with their start and end apart: 5, of which 4 were waited for; matrix products, arithmetic and copies ran while one was open for 11% of the time, Pallas kernels for 0%

profile of v1, /device:TPU:1, one launch (start us, length us, event | category | flops | bytes accessed | tf_op | source)
XLA Modules:
  0.0 492.6 jit_solution(13732701123297076356)
XLA Ops:
  7.2 2.1 stack.2
  9.2 6.7 %all-to-all-start = ((bf16[4,8,24,608]{3,2,1,0:T(8,128)(2,1)}), bf16[4,8,24,608]{3,2,1,0:T(8,128)(2,1)S(1)}, u32[]{:S(2)}, u32[]{:S(2)}) async-start(bf16[4,8,24,608]{3,2,1,0:T(8,128)(2,1)} %stack.2), calls=%async_computation | async-start | bytes 1966080 | tf_op jit(solution)/shard_map/all_to_all | solution.py:16
  16.0 0.7 all-gather.9.cloned.1.call-update
  16.7 1.0 copy.72
  17.8 19.4 %all_gather.12 = bf16[8,2,2432]{0,1,2:T(2,128)(2,1)S(1)} all-gather(bf16[8,2,608]{0,1,2:T(2,128)(2,1)S(1)} %copy.72), channel_id=1, replica_groups=mesh['row'=64,'col'=4] {'col'}, dimensions={2}, use_global_device_ids=true | all-gather | bytes 97280 | tf_op jit(solution)/shard_map/all_gather | solution.py:77
  37.2 1.1 copy.73
  38.4 0.1 fusion.70
  38.5 0.2 fusion.36
  38.7 3.2 fusion.19
  42.5 0.9 add_bitcast_fusion
  43.5 0.2 fusion.22
  43.8 0.4 multiply_reduce_fusion
  44.3 0.1 convert_bitcast_fusion
  44.4 1.3 copy.71
  45.7 2.3 reshape.214
  48.0 2.0 fusion.15
  50.0 4.8 convolution_bitcast_fusion.1
  54.8 0.2 slice_multiply_fusion.1
  55.0 0.8 copy-done.2
  55.8 0.2 copy.78
  56.3 0.3 mul.264
  56.5 0.2 mul.265
  56.8 0.3 fusion.33
  57.0 0.7 pad_maximum_fusion.1
  57.8 1.0 slice.80
  58.9 0.7 pad_maximum_fusion
  59.7 0.2 reduce-scatter.4.cloned.1.call-start
  60.1 0.2 reshape_squeeze.11
  60.2 0.2 copy.82
  60.6 40.6 %all-gather.9.cloned.1.call-done = bf16[64,38,512]{2,1,0:T(8,128)(2,1)} async-done(((bf16[1,38,512]{2,1,0:T(8,128)(2,1)}), bf16[64,38,512]{2,1,0:T(8,128)(2,1)}) %all-gather.9.cloned.1.call-update) | async-done | bytes 2490384 | tf_op jit(solution)/shard_map/all_gather | solution.py:119
  101.2 2.8 reshape.216
  104.0 137.7 %all-gather.7.cloned.1.call-done = bf16[8,1664,512]{2,0,1:T(8,128)(2,1)} async-done(((bf16[8,26,512]{2,0,1:T(8,128)(2,1)}), bf16[8,1664,512]{2,0,1:T(8,128)(2,1)}) %all-gather.7.cloned.1.call-update) | async-done | bytes 13631504 | tf_op jit(solution)/shard_map/all_gather | solution.py:101
  241.8 19.4 %copy.81 = bf16[8,1664,512]{1,2,0:T(8,128)(2,1)} copy(bf16[8,1664,512]{2,0,1:T(8,128)(2,1)} %all-gather.7.cloned.1.call-done) | data formatting | bytes 27262976 | tf_op jit(solution)/shard_map/all_gather | solution.py:101
  261.1 8.8 %fusion.71 = (f32[8,24,8]{1,2,0:T(8,128)S(1)}, bf16[8,24,8,1664]{3,1,2,0:T(8,128)(2,1)}) fusion(pred[8,1664]{1,0:T(8,128)(4,1)S(1)} %compare_or_fusion, bf16[8,1664,8,64]{1,3,2,0:T(8,128)(2,1)} %bitcast.120, f32[8,24,8,64]{3,2,1,0:T(8,128)S(1)} %reshape_squeeze.11, f32[64]{0:T(128)S(1)} %get-tuple-element.23, f32[8,24,8]{1,2,0:T(8,128)S(1)} %copy.83), kind=kOutput, calls=%fused_computation.106 | convolution fusion | flops 342787712 | bytes 19162368 | tf_op jit(solution)/shard_map/sub | solution.py:44
  270.0 122.4 %all-gather.5.cloned.1.call-done = bf16[8,1664,512]{2,0,1:T(8,128)(2,1)} async-done(((bf16[8,26,512]{2,0,1:T(8,128)(2,1)}), bf16[8,1664,512]{2,0,1:T(8,128)(2,1)}) %all-gather.5.cloned.1.call-update) | async-done | bytes 13631504 | tf_op jit(solution)/shard_map/all_gather | solution.py:102
  392.4 19.4 %copy.77 = bf16[8,1664,512]{1,2,0:T(8,128)(2,1)} copy(bf16[8,1664,512]{2,0,1:T(8,128)(2,1)} %all-gather.5.cloned.1.call-done) | data formatting | bytes 27262976 | tf_op jit(solution)/shard_map/all_gather | solution.py:102
  411.8 8.4 %fusion.26 = bf16[8,24,8,64]{3,1,2,0:T(8,128)(2,1)S(1)} fusion(bf16[8,1664,8,64]{1,3,2,0:T(8,128)(2,1)} %bitcast.121, bf16[8,24,8,1664]{3,1,2,0:T(8,128)(2,1)} %get-tuple-element.27, f32[8,24,8]{1,2,0:T(8,128)S(1)} %get-tuple-element.26), kind=kOutput, calls=%fused_computation.26 | convolution fusion | flops 327352320 | bytes 18946048 | tf_op jit(solution)/shard_map/rqhk,rkhd->rqhd/dot_general | solution.py:46
  420.3 0.3 reshape.210
  420.6 2.3 convolution_bitcast_fusion
  422.9 0.9 dynamic-slice_bitcast_fusion.1
  423.8 42.7 %reduce-scatter.4.cloned.1.call-done = f32[608,192]{1,0:T(8,128)} async-done(((f32[2432,192]{1,0:T(8,128)}), f32[608,192]{1,0:T(8,128)}) %reduce-scatter.4.cloned.1.call-update) | async-done | bytes 466960
  466.4 1.3 copy.90
  467.8 0.2 fusion.40
  467.9 5.5 %all-reduce = (f32[8,24]{1,0:T(8,128)S(1)}, f32[8,24]{1,0:T(8,128)S(1)}) all-reduce(f32[8,24]{1,0:T(8,128)S(1)} %get-tuple-element.3, f32[8,24]{1,0:T(8,128)S(1)} %get-tuple-element.2), channel_id=1, replica_groups=mesh['row'=64,'col'=4] {'col'}, use_global_device_ids=true, to_apply=%region_13.14 | all-reduce | flops 384 | bytes 3072 | tf_op jit(solution)/shard_map/psum | solution.py:129
  473.4 0.2 add_convert_fusion
  473.6 0.2 fusion.76
  473.9 11.5 %psum.23 = f32[8,24,64]{2,1,0:T(8,128)S(1)} all-reduce(f32[8,24,64]{2,1,0:T(8,128)S(1)} %bitcast.130), channel_id=1, replica_groups=mesh['row'=64,'col'=4] {'col'}, use_global_device_ids=true, to_apply=%region_14.15 | all-reduce | flops 12288 | bytes 98304 | tf_op jit(solution)/shard_map/psum | solution.py:134
  485.3 0.8 multiply_subtract_fusion
  (58 shorter events, 1.6 us)
Async XLA Ops:
  7.2 466.5 %copy-start = (bf16[608,64]{0,1:T(8,128)(2,1)S(1)}, bf16[608,64]{0,1:T(8,128)(2,1)}, u32[]{:S(2)}) copy-start(bf16[608,64]{0,1:T(8,128)(2,1)} %param.20) | copy-start | bytes 233476
  7.2 31.2 %copy-start.3 = (f32[8,2,2432]{2,1,0:T(2,128)S(1)}, f32[8,2,2432]{2,1,0:T(2,128)}, u32[]{:S(2)}) copy-start(f32[8,2,2432]{2,1,0:T(2,128)} %param.16) | copy-start | bytes 466948
  9.2 34.2 %all-to-all-start = ((bf16[4,8,24,608]{3,2,1,0:T(8,128)(2,1)}), bf16[4,8,24,608]{3,2,1,0:T(8,128)(2,1)S(1)}, u32[]{:S(2)}, u32[]{:S(2)}) async-start(bf16[4,8,24,608]{3,2,1,0:T(8,128)(2,1)} %stack.2), calls=%async_computation | async-start | bytes 1966080 | tf_op jit(solution)/shard_map/all_to_all | solution.py:16
  16.0 26.4 %copy-start.5 = (f32[3,64]{1,0:T(4,128)S(1)}, f32[3,64]{1,0:T(4,128)}, u32[]{:S(2)}) copy-start(f32[3,64]{1,0:T(4,128)} %param.21) | copy-start | bytes 2308
  16.0 85.3 %all-gather.9.cloned.1.call-start = ((), (), s32[]{:S(2)}) async-start(), calls=%async_computation.4 | async-start | bytes 2662400 | tf_op jit(solution)/shard_map/all_gather | solution.py:119
  16.7 225.1 %all-gather.7.cloned.1.call-start = ((), (), s32[]{:S(2)}) async-start(), calls=%async_computation.3 | async-start | bytes 13844480 | tf_op jit(solution)/shard_map/all_gather | solution.py:101
  54.8 1.0 copy-start.2
  54.8 5.2 %copy-start.6 = (s32[8]{0:T(128)S(1)}, s32[8]{0:T(128)}, u32[]{:S(2)}) copy-start(s32[8]{0:T(128)} %param.22) | copy-start | bytes 100
  57.8 334.6 %all-gather.5.cloned.1.call-start = ((), (), s32[]{:S(2)}) async-start(), calls=%async_computation.2 | async-start | bytes 13844480 | tf_op jit(solution)/shard_map/all_gather | solution.py:102
  59.7 406.8 %reduce-scatter.4.cloned.1.call-start = ((), (), s32[]{:S(2)}) async-start(), calls=%async_computation.5 | async-start | bytes 3112960
  420.3 3.5 copy-start.7
  420.5 47.2 %copy-start.1 = (bf16[8,24,608]{2,1,0:T(8,128)(2,1)S(1)}, bf16[8,24,608]{2,1,0:T(8,128)(2,1)}, u32[]{:S(2)}) copy-start(bf16[8,24,608]{2,1,0:T(8,128)(2,1)} %param.12) | copy-start | bytes 700420
  420.5 64.8 %copy-start.4 = (f32[8,24,64]{2,1,0:T(8,128)S(1)}, f32[8,24,64]{2,1,0:T(8,128)}, u32[]{:S(2)}) copy-start(f32[8,24,64]{2,1,0:T(8,128)} %param.14) | copy-start | bytes 147460
Sparse Core Ops, SparseCore 0:
  20.1 81.0 all-gather.8
  104.5 137.1 all-gather.6
  245.1 147.3 all-gather.4
  423.0 43.4 reduce-scatter.3
